TPU v7x, 256 devices: a whole 4x4x8 slice. The times are simulated.
256 devices in a mesh: space: 64 (over z, x, core), head: 4 (over y).
Axes of the slice: x: 4, y: 4, z: 8, core: 2. Of those that a mesh axis runs over, the one named last changes fastest.
Arguments:
- features: bfloat16 [512, 16, 16, 128], P('space', None, None, 'head'), may hold values from -6 to 6
- mask: int32 [512, 16, 16], P('space'), may hold values from 0 to 1, as said below
- conv1_weight: bfloat16 [27, 128, 128], replicated, may hold values from -0.21875 to 0.21875
- conv2_weight: bfloat16 [27, 128, 128], replicated, may hold values from -0.21875 to 0.21875
- down_weight: bfloat16 [8, 128, 512], replicated, may hold values from -0.1875 to 0.1875
- norm_gain: float32 [512], replicated, may hold values from 0.1 to 1.9
- qkv_weight: bfloat16 [512, 3, 512], P(None, None, 'head'), may hold values from -2 to 2
- out_weight: bfloat16 [512, 512], P('head'), may hold values from -0.25 to 0.25
Outputs:
- refined: bfloat16 [512, 16, 16, 128], P('space', None, None, 'head')
- level_out: bfloat16 [16384, 512], P('space', 'head')
Inputs may be any that keep to these rules, and one draw needn't show every extreme that they name: `mask`: A voxel is occupied only inside an active brick of 8^3 aligned voxels; the first brick and its first voxel are always occupied.
All inputs are finite; a program needn't handle non-finite values.
Results may differ from a plain program's by a relative error of at most 0.012.
Values may be sent and summed in bfloat16 or wider, within the bound.
No kernel may reach another device: no remote copies, remote signals or barrier semaphores. Data moves between devices by JAX's collectives and lax.ppermute only.
A program may use at most 64 MiB of HBM per device.

v0:
```python
import jax
import jax.numpy as jnp
from jax import lax
from jax.sharding import PartitionSpec as P

HEADS = 8
KEY_BLOCK = 1024


def with_halo(cells, axis, width):
    count = lax.axis_size(axis)
    ends = count - 1
    head = lax.slice_in_dim(cells, 0, width, axis=0)
    tail = lax.slice_in_dim(cells, cells.shape[0] - width, cells.shape[0], axis=0)
    return jnp.concatenate(
        [
            lax.ppermute(tail, axis, [(i, i + 1) for i in range(ends)]),
            cells,
            lax.ppermute(head, axis, [(i + 1, i) for i in range(ends)]),
        ],
        axis=0,
    )


def convolve(rimmed, weight):
    chans = weight.shape[1]
    kernel = weight.reshape(3, 3, 3, chans, weight.shape[2])
    out = lax.conv_general_dilated(
        rimmed[None],
        kernel,
        window_strides=(1, 1, 1),
        padding=((0, 0), (1, 1), (1, 1)),
        dimension_numbers=("NDHWC", "DHWIO", "NDHWC"),
        preferred_element_type=jnp.float32,
    )
    return out[0]


def to_cells(field):
    nx, ny, nz, count = field.shape
    blocks = field.reshape(nx // 2, 2, ny // 2, 2, nz // 2, 2, count).transpose(0, 2, 4, 1, 3, 5, 6)
    return blocks.reshape(nx // 2 * (ny // 2) * (nz // 2), 8 * count)


def body(
    features, mask, conv1_weight, conv2_weight, down_weight, norm_gain, qkv_weight, out_weight
):
    member = lax.axis_index("head")
    nx, ny, nz, local = features.shape
    width = down_weight.shape[2]
    chans = conv1_weight.shape[1]
    tokens = nx // 2 * (ny // 2) * (nz // 2)
    occupied = mask.astype(jnp.float32)[..., None]
    masked = features * mask.astype(jnp.bfloat16)[..., None]
    rimmed = lax.all_gather(with_halo(masked, "space", 1), "head", axis=3, tiled=True)
    whole_masked = lax.slice_in_dim(rimmed, 1, nx + 1, axis=0)
    pre1 = convolve(rimmed, conv1_weight)
    hidden = (occupied * jax.nn.silu(pre1)).astype(jnp.bfloat16)
    pre2 = convolve(with_halo(hidden, "space", 1), conv2_weight)
    refined_all = (occupied * (whole_masked.astype(jnp.float32) + pre2)).astype(jnp.bfloat16)
    refined = lax.dynamic_slice_in_dim(refined_all, member * local, local, 3)
    coarse = jnp.dot(
        to_cells(refined_all),
        down_weight.reshape(8 * chans, width),
        preferred_element_type=jnp.float32,
    ).astype(jnp.bfloat16)
    wide = coarse.astype(jnp.float32)
    normed = (
        wide * lax.rsqrt(jnp.mean(wide * wide, axis=1, keepdims=True) + 1e-05) * norm_gain
    ).astype(jnp.bfloat16)
    local_cols = qkv_weight.shape[2]
    proj = jnp.dot(
        normed, qkv_weight.reshape(width, 3 * local_cols), preferred_element_type=jnp.float32
    )
    proj = proj.astype(jnp.bfloat16).reshape(tokens, 3, local_cols)
    head_size = width // HEADS
    heads_here = local_cols // head_size
    query = proj[:, 0].reshape(tokens, heads_here, head_size)
    live_cell = (
        mask.reshape(nx // 2, 2, ny // 2, 2, nz // 2, 2)
        .max(axis=(1, 3, 5))
        .reshape(1, -1)
        .astype(jnp.bfloat16)
    )
    span = 2 * local_cols
    live_len = -(-tokens // span) * span
    live_rows = jnp.pad(live_cell, ((0, 0), (0, live_len - tokens))).reshape(-1, span)
    live_count = live_rows.shape[0]
    live_rows = jnp.pad(live_rows, ((0, -(-live_count // 8) * 8 - live_count), (0, 0)))
    piece = jnp.concatenate([proj[:, 1], proj[:, 2]], axis=1)
    piece = jnp.concatenate([piece, live_rows], axis=0)
    rows = piece.shape[0]
    gathered = lax.all_gather(piece[None], "space", axis=0, tiled=True)
    parts = gathered.shape[0]
    count = parts * tokens
    piece_keys = gathered[:, :tokens, :local_cols].reshape(count, heads_here, head_size)
    piece_values = gathered[:, :tokens, local_cols:].reshape(count, heads_here, head_size)
    piece_live = (
        gathered[:, tokens : tokens + live_count].reshape(parts, -1)[:, :tokens].reshape(count)
    )
    bias = jnp.where(piece_live > 0, 0.0, -1e30).astype(jnp.float32)
    scale = head_size ** (-0.5)

    def one_block(carry, block):
        top_old, sums, accum = carry
        block_keys, block_values, block_bias = block
        scores = (
            jnp.einsum("qhd,khd->hqk", query, block_keys, preferred_element_type=jnp.float32)
            * scale
            + block_bias[None, None, :]
        )
        top_new = jnp.maximum(top_old, jnp.max(scores, axis=-1))
        expo = jnp.exp(scores - top_new[..., None])
        factor = jnp.exp(top_old - top_new)
        sums = sums * factor + jnp.sum(expo, axis=-1)
        accum = accum * factor[..., None] + jnp.einsum(
            "hqk,khd->hqd",
            expo.astype(jnp.bfloat16),
            block_values,
            preferred_element_type=jnp.float32,
        )
        return ((top_new, sums, accum), None)

    start_state = (
        jnp.full((heads_here, tokens), -1e30, jnp.float32),
        jnp.zeros((heads_here, tokens), jnp.float32),
        jnp.zeros((heads_here, tokens, head_size), jnp.float32),
    )
    size = KEY_BLOCK if count % KEY_BLOCK == 0 else tokens
    blocks = count // size
    stacked = (
        piece_keys.reshape(blocks, size, heads_here, head_size),
        piece_values.reshape(blocks, size, heads_here, head_size),
        bias.reshape(blocks, size),
    )
    carry, unused = lax.scan(one_block, start_state, stacked)
    top_final, sums, accum = carry
    attn = (
        (accum / sums[..., None])
        .transpose(1, 0, 2)
        .reshape(tokens, local_cols)
        .astype(jnp.bfloat16)
    )
    cols_w = lax.all_to_all(out_weight, "head", 1, 0, tiled=True)
    attn_all = lax.all_gather(attn, "head", axis=1, tiled=True)
    mixed = jnp.dot(attn_all, cols_w, preferred_element_type=jnp.float32)
    mine = lax.dynamic_slice_in_dim(wide, member * local_cols, local_cols, 1)
    level_out = (mine + mixed).astype(jnp.bfloat16)
    return (refined, level_out)


def solution(mesh):
    in_specs = (
        P("space", None, None, "head"),
        P("space", None, None),
        P(),
        P(),
        P(),
        P(),
        P(None, None, "head"),
        P("head", None),
    )
    out_specs = (P("space", None, None, "head"), P("space", "head"))
    return jax.shard_map(body, mesh=mesh, in_specs=in_specs, out_specs=out_specs, check_vma=False)
```

profile of v0, /device:TPU:8, one launch (start us, length us, event | category | flops | bytes accessed | tf_op | source)
XLA Modules:
  0.0 343.7 jit_solution(4440227885603397588)
XLA Ops:
  7.2 1.0 fusion.60
  8.2 2.7 copy.59
  11.1 1.7 collective-permute-start
  12.8 1.3 collective-permute-start.1
  14.2 3.1 collective-permute-done.1
  17.6 45.3 %all_gather.9 = bf16[10,16,16,128]{2,1,0,3:T(8,128)(2,1)} all-gather(bf16[10,16,16,32]{2,1,0,3:T(8,128)(2,1)S(1)} %pad_maximum_fusion), channel_id=1, replica_groups=mesh['space'=64,'head'=4] {'head'}, dimensions={3}, use_global_device_ids=true | all-gather | bytes 819200 | tf_op jit(solution)/shard_map/all_gather | solution.py:55
  62.9 5.2 %copy.60 = bf16[10,16,16,128]{3,1,2,0:T(8,128)(2,1)S(1)} copy(bf16[10,16,16,128]{2,1,0,3:T(8,128)(2,1)} %all_gather.9) | data formatting | bytes 1310720 | tf_op jit(solution)/shard_map/all_gather | solution.py:55
  68.8 0.5 copy-done.5
  69.3 6.2 %fusion.35 = f32[8,16,8,3,128]{4,2,3,1,0:T(8,128)S(1)} fusion(bf16[3,3,3,128,128]{4,3,2,1,0:T(8,128)(2,1)S(1)} %bitcast.110, bf16[10,16,1,7,2,128]{5,3,4,1,0,2:T(8,128)(2,1)S(1)} %slice.51, bf16[10,16,1,8,3,128]{5,3,4,1,0,2:T(8,128)(2,1)S(1)} %copy.63, pred[8,3]{0,1:T(4,128)(4,1)S(1)} %copy-done.7), kind=kOutput, calls=%fused_computation.40 | convolution fusion | flops 2609971200 | bytes 4014104 | tf_op jit(solution)/shard_map/conv_general_dilated | solution.py:28
  76.1 4.3 %collective-permute-start.2 = (bf16[1,16,16,128]{3,1,2,0:T(8,128)(2,1)S(1)}, bf16[1,16,16,128]{3,1,2,0:T(8,128)(2,1)S(1)}, u32[]{:S(2)}, u32[]{:S(2)}) collective-permute-start(bf16[1,16,16,128]{3,1,2,0:T(8,128)(2,1)S(1)} %get-tuple-element.128), channel_id=1, source_target_pairs={{0,4},{4,8},{8,12},{12,16},{16,20},{20,24},{24,28},{28,32},{32,36}... | collective-permute-start | bytes 196616 | tf_op jit(solution)/shard_map/ppermute | solution.py:17
  80.5 1.5 collective-permute-start.3
  82.1 1.2 copy.69
  83.3 0.6 reduce_max.18
  84.1 1.9 collective-permute-done.3
  86.7 0.5 copy-done.6
  87.2 6.2 %fusion.32 = f32[8,16,8,3,128]{4,2,3,1,0:T(8,128)S(1)} fusion(bf16[3,3,3,128,128]{4,3,2,1,0:T(8,128)(2,1)S(1)} %bitcast.111, bf16[10,16,1,7,2,128]{5,3,4,1,0,2:T(8,128)(2,1)S(1)} %slice.55, bf16[10,16,1,8,3,128]{5,3,4,1,0,2:T(8,128)(2,1)S(1)} %copy.66, pred[8,3]{0,1:T(4,128)(4,1)S(1)} %copy-done.7), kind=kOutput, calls=%fused_computation.39 | convolution fusion | flops 2609971200 | bytes 4014104 | tf_op jit(solution)/shard_map/conv_general_dilated | solution.py:28
  94.4 0.5 multiply_reduce_fusion
  95.5 0.8 copy.74
  96.3 0.8 copy.79
  97.1 4.5 %all-to-all-start = ((bf16[128,4,128]{0,2,1:T(8,128)(2,1)}), bf16[128,4,128]{0,2,1:T(8,128)(2,1)S(1)}, u32[]{:S(2)}, u32[]{:S(2)}) async-start(bf16[128,4,128]{0,2,1:T(8,128)(2,1)} %bitcast.24), calls=%async_computation | async-start | bytes 262144 | tf_op jit(solution)/shard_map/all_to_all | solution.py:144
  101.8 0.9 copy.81
  102.7 3.4 all-to-all-done
  106.2 82.1 %all-gather.3.cloned.1.call-done = bf16[16896,256]{1,0:T(8,128)(2,1)} async-done(((bf16[264,256]{1,0:T(8,128)(2,1)}), bf16[16896,256]{1,0:T(8,128)(2,1)}) %all-gather.3.cloned.1.call-update) | async-done | bytes 8650768 | tf_op jit(solution)/shard_map/all_gather | solution.py:93
  188.3 1.1 fusion.49
  189.5 6.0 %fusion.56 = (bf16[64,256,128]{2,1,0:T(8,128)(2,1)}, bf16[64,256,128]{2,1,0:T(8,128)(2,1)}) fusion(bf16[64,264,256]{2,1,0:T(8,128)(2,1)} %bitcast.93), kind=kLoop, calls=%fused_computation.77 | loop fusion | bytes 16777216 | tf_op jit(solution)/shard_map/slice | solution.py:97
  195.5 14.7 %reshape.108 = bf16[16,1024,2,64]{3,2,1,0:T(2,128)(2,1)} reshape(bf16[64,256,128]{2,1,0:T(8,128)(2,1)} %get-tuple-element.124) | data formatting | bytes 8388608 | tf_op jit(solution)/shard_map/reshape;reshape | solution.py:133
  210.2 20.1 %copy.78 = bf16[16,1024,2,64]{1,3,2,0:T(8,128)(2,1)} copy(bf16[16,1024,2,64]{3,2,1,0:T(2,128)(2,1)} %reshape.108) | data formatting | bytes 8388608
  230.3 14.7 %reshape.107 = bf16[16,1024,2,64]{3,2,1,0:T(2,128)(2,1)} reshape(bf16[64,256,128]{2,1,0:T(8,128)(2,1)} %get-tuple-element.125) | data formatting | bytes 8388608 | tf_op jit(solution)/shard_map/reshape;reshape | solution.py:132
  245.0 20.1 %copy.77 = bf16[16,1024,2,64]{1,3,2,0:T(8,128)(2,1)} copy(bf16[16,1024,2,64]{3,2,1,0:T(2,128)(2,1)} %reshape.107) | data formatting | bytes 8388608
  265.1 58.0 %while.15 = (s32[]{:T(128)}, f32[2,256]{1,0:T(2,128)S(1)}, f32[2,256]{1,0:T(2,128)S(1)}, f32[2,256,64]{1,2,0:T(8,128)S(1)}, bf16[16,1024,2,64]{1,3,2,0:T(8,128)(...) while((s32[]{:T(128)}, f32[2,256]{1,0:T(2,128)S(1)}, ...), condition=%wide.region_5.6_spmd.clone, body=%wide.region_2.5_spmd.clone.sunk | while | flops 140085760 | bytes 7196805 | solution.py:136
  265.1 1.5 bitcast_reduce_fusion.2
  267.1 1.6 convolution_add_fusion.3
  268.7 1.5 bitcast_reduce_fusion.2
  270.7 1.6 convolution_add_fusion.3
  272.4 1.5 bitcast_reduce_fusion.2
  274.4 1.6 convolution_add_fusion.3
  276.0 1.5 bitcast_reduce_fusion.2
  278.0 1.6 convolution_add_fusion.3
  279.6 1.5 bitcast_reduce_fusion.2
  281.6 1.6 convolution_add_fusion.3
  283.3 1.5 bitcast_reduce_fusion.2
  285.3 1.6 convolution_add_fusion.3
  286.9 1.5 bitcast_reduce_fusion.2
  288.9 1.6 convolution_add_fusion.3
  290.5 1.5 bitcast_reduce_fusion.2
  292.5 1.6 convolution_add_fusion.3
  294.1 1.5 bitcast_reduce_fusion.2
  296.1 1.6 convolution_add_fusion.3
  297.8 1.5 bitcast_reduce_fusion.2
  299.8 1.6 convolution_add_fusion.3
  301.4 1.5 bitcast_reduce_fusion.2
  303.4 1.6 convolution_add_fusion.3
  305.0 1.5 bitcast_reduce_fusion.2
  307.0 1.6 convolution_add_fusion.3
  308.7 1.5 bitcast_reduce_fusion.2
  310.7 1.6 convolution_add_fusion.3
  312.3 1.5 bitcast_reduce_fusion.2
  314.3 1.6 convolution_add_fusion.3
  315.9 1.5 bitcast_reduce_fusion.2
  317.9 1.6 convolution_add_fusion.3
  319.5 1.5 bitcast_reduce_fusion.2
  321.6 1.6 convolution_add_fusion.3
  323.2 12.8 %all_gather.11 = bf16[256,512]{0,1:T(8,128)(2,1)S(1)} all-gather(bf16[256,128]{0,1:T(8,128)(2,1)S(1)} %bitcast.109), channel_id=1, replica_groups=mesh['space'=64,'head'=4] {'head'}, dimensions={1}, use_global_device_ids=true | all-gather | bytes 327680 | tf_op jit(solution)/shard_map/all_gather | solution.py:145
  336.0 0.9 fusion.39
  (130 shorter events, 13.2 us)
Async XLA Ops:
  7.2 87.3 %copy-start = (bf16[8,128,512]{2,1,0:T(8,128)(2,1)S(1)}, bf16[8,128,512]{2,1,0:T(8,128)(2,1)}, u32[]{:S(2)}) copy-start(bf16[8,128,512]{2,1,0:T(8,128)(2,1)} %param.14) | copy-start | bytes 3145732
  7.2 181.2 %all-gather.3.cloned.1.call-start = ((), (), s32[]{:S(2)}) async-start(), calls=%async_computation.1 | async-start | bytes 8785920 | tf_op jit(solution)/shard_map/all_gather | solution.py:93
  11.1 3.1 collective-permute-start
  12.8 4.5 %collective-permute-start.1 = (bf16[1,16,16,32]{2,1,0,3:T(8,128)(2,1)S(1)}, bf16[1,16,16,32]{2,1,0,3:T(8,128)(2,1)S(1)}, u32[]{:S(2)}, u32[]{:S(2)}) collective-permute-start(bf16[1,16,16,32]{2,1,0,3:T(8,128)(2,1)S(1)} %get-tuple-element.127), channel_id=1, source_target_pairs={{4,0},{8,4},{12,8},{16,12},{20,16},{24,20},{28,24},{32,28},{36,32}... | collective-permute-start | bytes 49160 | tf_op jit(solution)/shard_map/ppermute | solution.py:19
  68.1 1.2 copy-start.5
  68.1 1.2 copy-start.7
  75.5 6.5 %copy-start.2 = (s32[8,16,16]{2,1,0:T(8,128)S(1)}, s32[8,16,16]{2,1,0:T(8,128)}, u32[]{:S(2)}) copy-start(s32[8,16,16]{2,1,0:T(8,128)} %param.11) | copy-start | bytes 24580
  76.1 7.9 %collective-permute-start.2 = (bf16[1,16,16,128]{3,1,2,0:T(8,128)(2,1)S(1)}, bf16[1,16,16,128]{3,1,2,0:T(8,128)(2,1)S(1)}, u32[]{:S(2)}, u32[]{:S(2)}) collective-permute-start(bf16[1,16,16,128]{3,1,2,0:T(8,128)(2,1)S(1)} %get-tuple-element.128), channel_id=1, source_target_pairs={{0,4},{4,8},{8,12},{12,16},{16,20},{20,24},{24,28},{28,32},{32,36}... | collective-permute-start | bytes 196616 | tf_op jit(solution)/shard_map/ppermute | solution.py:17
  80.5 5.5 %collective-permute-start.3 = (bf16[1,16,16,128]{3,1,2,0:T(8,128)(2,1)S(1)}, bf16[1,16,16,128]{3,1,2,0:T(8,128)(2,1)S(1)}, u32[]{:S(2)}, u32[]{:S(2)}) collective-permute-start(bf16[1,16,16,128]{3,1,2,0:T(8,128)(2,1)S(1)} %get-tuple-element.129), channel_id=1, source_target_pairs={{4,0},{8,4},{12,8},{16,12},{20,16},{24,20},{28,24},{32,28},{36,32}... | collective-permute-start | bytes 196616 | tf_op jit(solution)/shard_map/ppermute | solution.py:19
  86.0 1.2 copy-start.6
  94.1 0.9 copy-start.4
  94.4 1.9 copy-start.3
  97.1 9.0 %all-to-all-start = ((bf16[128,4,128]{0,2,1:T(8,128)(2,1)}), bf16[128,4,128]{0,2,1:T(8,128)(2,1)S(1)}, u32[]{:S(2)}, u32[]{:S(2)}) async-start(bf16[128,4,128]{0,2,1:T(8,128)(2,1)} %bitcast.24), calls=%async_computation | async-start | bytes 262144 | tf_op jit(solution)/shard_map/all_to_all | solution.py:144
  323.1 13.7 %copy-start.1 = (bf16[8,128,512]{2,1,0:T(8,128)(2,1)S(1)}, bf16[8,128,512]{2,1,0:T(8,128)(2,1)}, u32[]{:S(2)}) copy-start(bf16[8,128,512]{2,1,0:T(8,128)(2,1)} %param.14) | copy-start | bytes 3145732
Sparse Core Ops, SparseCore 0:
  96.4 91.8 all-gather.2
where the time goes:
time: 347 us; the launch traced here: 344 us
  local copies, waits for them, and re-layouts  91.5 us (26%)
  waiting for transfers between devices  90.5 us (26%)
  matrix products  62.8 us (18%)
  blocking collectives  58.1 us (17%)
  between operations  14.4 us (4%)
  starting transfers between devices  13.4 us (4%)
  other arithmetic  12.2 us (4%)
    all_gather x1, waiting for transfers between devices, body(): gathered = lax.all_gather(piece[None], 'space', axis=0, tiled=True)  82.1 us
    unnamed x22, local copies, waits for them, and re-layouts  46.9 us
    all_gather x1, blocking collectives, body(): lax.all_gather(with_halo(masked, 'space', 1), 'head', axis=3, tiled=True)  45.3 us
    dot_general x16, matrix products, one_block(): jnp.einsum('hqk,khd->hqd', expo.astype(jnp.bfloat16), block_values, prefe...  25.1 us
    dot_general x16, matrix products, one_block(): jnp.einsum('qhd,khd->hqk', query, block_keys, preferred_element_type=jnp....  23.6 us
    another operation x1, local copies, waits for them, and re-layouts, body(): piece_values.reshape(blocks, size, heads_here, head_size)  14.7 us
    another operation x1, local copies, waits for them, and re-layouts, body(): piece_keys.reshape(blocks, size, heads_here, head_size)  14.7 us
    all_gather x1, blocking collectives, body(): attn_all = lax.all_gather(attn, 'head', axis=1, tiled=True)  12.8 us
  transfers between devices with their start and end apart: 6, of which 4 were waited for; matrix products, arithmetic and copies ran while one was open for 1% of the time, Pallas kernels for 0%

commit v1 on v0

--- a/solution.py
+++ b/solution.py
@@ -90,7 +90,11 @@
     piece = jnp.concatenate([proj[:, 1], proj[:, 2]], axis=1)
     piece = jnp.concatenate([piece, live_rows], axis=0)
     rows = piece.shape[0]
-    gathered = lax.all_gather(piece[None], "space", axis=0, tiled=True)
+    part = piece[None]
+    devices = lax.axis_size("space")
+    pieces = jnp.stack([part for _ in range(devices)])
+    pieces = lax.all_to_all(pieces, "space", split_axis=0, concat_axis=0)
+    gathered = jnp.concatenate(pieces, axis=0)
     parts = gathered.shape[0]
     count = parts * tokens
     piece_keys = gathered[:, :tokens, :local_cols].reshape(count, heads_here, head_size)

time: 347 us -> 459 us (1.32)
  waiting for transfers between devices: 90.5 us -> 193 us
  starting transfers between devices: 13.4 us -> 31.5 us
  between operations: 14.4 us -> 1.08 us
    all_to_all x0 -> x1, waiting for transfers between devices: none -> 190 us  [body(): pieces = lax.all_to_all(pieces, 'space', split_axis=0, concat_axis=0)]
    all_gather x1 -> x0, waiting for transfers between devices: 82.1 us -> none  [body(): gathered = lax.all_gather(piece[None], 'space', axis=0, tiled=True)]
    all_to_all x0 -> x1, starting transfers between devices: none -> 18.4 us  [body(): pieces = lax.all_to_all(pieces, 'space', split_axis=0, concat_axis=0)]
    unnamed x22 -> x24, local copies, waits for them, and re-layouts: 46.9 us -> 46.9 us
  transfers between devices with their start and end apart: 6 -> 6, of which waited for: 4 -> 2; matrix products, arithmetic and copies ran while one was open for 1% -> 3% of each run, Pallas kernels for 0% -> 0%
where the time goes in v1:
time: 459 us; the launch traced here: 455 us
  waiting for transfers between devices  193 us (42%)
  local copies, waits for them, and re-layouts  95.5 us (21%)
  matrix products  62.8 us (14%)
  blocking collectives  57.7 us (13%)
  starting transfers between devices  31.5 us (7%)
  other arithmetic  12.2 us (3%)
    all_to_all x1, waiting for transfers between devices, body(): pieces = lax.all_to_all(pieces, 'space', split_axis=0, concat_axis=0)  190 us
    unnamed x24, local copies, waits for them, and re-layouts  46.9 us
    all_gather x1, blocking collectives, body(): lax.all_gather(with_halo(masked, 'space', 1), 'head', axis=3, tiled=True)  45.3 us
    dot_general x16, matrix products, one_block(): jnp.einsum('hqk,khd->hqd', expo.astype(jnp.bfloat16), block_values, prefe...  25.1 us
    dot_general x16, matrix products, one_block(): jnp.einsum('qhd,khd->hqk', query, block_keys, preferred_element_type=jnp....  23.6 us
    all_to_all x1, starting transfers between devices, body(): pieces = lax.all_to_all(pieces, 'space', split_axis=0, concat_axis=0)  18.4 us
    another operation x1, local copies, waits for them, and re-layouts, body(): piece_values.reshape(blocks, size, heads_here, head_size)  14.8 us
    another operation x1, local copies, waits for them, and re-layouts, body(): piece_keys.reshape(blocks, size, heads_here, head_size)  14.7 us
  transfers between devices with their start and end apart: 6, of which 2 were waited for; matrix products, arithmetic and copies ran while one was open for 3% of the time, Pallas kernels for 0%

profile of v1, /device:TPU:8, one launch (start us, length us, event | category | flops | bytes accessed | tf_op | source)
XLA Modules:
  0.0 455.0 jit_solution(8242564175500330522)
XLA Ops:
  0.6 1.0 fusion.60
  1.6 2.7 copy.56
  4.5 1.7 collective-permute-start
  6.2 1.3 collective-permute-start.1
  7.6 3.1 collective-permute-done.1
  11.0 45.3 %all_gather.6 = bf16[10,16,16,128]{2,1,0,3:T(8,128)(2,1)} all-gather(bf16[10,16,16,32]{2,1,0,3:T(8,128)(2,1)S(1)} %pad_maximum_fusion), channel_id=1, replica_groups=mesh['space'=64,'head'=4] {'head'}, dimensions={3}, use_global_device_ids=true | all-gather | bytes 819200 | tf_op jit(solution)/shard_map/all_gather | solution.py:55
  56.4 5.2 %copy.57 = bf16[10,16,16,128]{3,1,2,0:T(8,128)(2,1)S(1)} copy(bf16[10,16,16,128]{2,1,0,3:T(8,128)(2,1)} %all_gather.6) | data formatting | bytes 1310720 | tf_op jit(solution)/shard_map/all_gather | solution.py:55
  62.2 0.5 copy-done.5
  62.7 6.2 %fusion.35 = f32[8,16,8,3,128]{4,2,3,1,0:T(8,128)S(1)} fusion(bf16[3,3,3,128,128]{4,3,2,1,0:T(8,128)(2,1)S(1)} %bitcast.108, bf16[10,16,1,7,2,128]{5,3,4,1,0,2:T(8,128)(2,1)S(1)} %slice.51, bf16[10,16,1,8,3,128]{5,3,4,1,0,2:T(8,128)(2,1)S(1)} %copy.60, pred[8,3]{0,1:T(4,128)(4,1)S(1)} %copy-done.7), kind=kOutput, calls=%fused_computation.40 | convolution fusion | flops 2609971200 | bytes 4014104 | tf_op jit(solution)/shard_map/conv_general_dilated | solution.py:28
  69.6 0.6 fusion.58
  70.2 4.3 collective-permute-start.2
  74.5 1.3 collective-permute-start.3
  75.8 0.8 copy.76
  76.6 4.5 all-to-all-start.1
  81.3 1.2 copy.66
  82.4 0.6 reduce_max.18
  84.0 0.5 copy-done.6
  84.5 6.2 %fusion.32 = f32[8,16,8,3,128]{4,2,3,1,0:T(8,128)S(1)} fusion(bf16[3,3,3,128,128]{4,3,2,1,0:T(8,128)(2,1)S(1)} %bitcast.109, bf16[10,16,1,7,2,128]{5,3,4,1,0,2:T(8,128)(2,1)S(1)} %slice.55, bf16[10,16,1,8,3,128]{5,3,4,1,0,2:T(8,128)(2,1)S(1)} %copy.63, pred[8,3]{0,1:T(4,128)(4,1)S(1)} %copy-done.8), kind=kOutput, calls=%fused_computation.39 | convolution fusion | flops 2609971200 | bytes 4014104 | tf_op jit(solution)/shard_map/conv_general_dilated | solution.py:28
  91.7 0.5 multiply_reduce_fusion
  92.9 3.9 stack.3
  96.8 18.4 %all-to-all-start = ((bf16[64,1,264,256]{3,2,1,0:T(8,128)(2,1)}), bf16[64,1,264,256]{3,2,1,0:T(8,128)(2,1)}, u32[]{:S(2)}, u32[]{:S(2)}) async-start(bf16[64,1,264,256]{3,2,1,0:T(8,128)(2,1)} %stack.3), calls=%async_computation | async-start | bytes 17301504 | tf_op jit(solution)/shard_map/all_to_all | solution.py:96
  115.4 0.9 copy.78
  116.5 190.3 %all-to-all-done = bf16[64,1,264,256]{3,2,1,0:T(8,128)(2,1)} async-done(((bf16[64,1,264,256]{3,2,1,0:T(8,128)(2,1)}), bf16[64,1,264,256]{3,2,1,0:T(8,128)(2,1)}, u32[]{:S(2)}, u32[]{:S(2)}) %all-to-all-start) | async-done | bytes 8650784 | tf_op jit(solution)/shard_map/all_to_all | solution.py:96
  306.8 1.1 fusion.49
  307.9 6.0 %fusion.56 = (bf16[64,256,128]{2,1,0:T(8,128)(2,1)}, bf16[64,256,128]{2,1,0:T(8,128)(2,1)}) fusion(bf16[64,264,256]{2,1,0:T(8,128)(2,1)} %bitcast.20), kind=kLoop, calls=%fused_computation.77 | loop fusion | bytes 16777216 | tf_op jit(solution)/shard_map/slice | solution.py:101
  313.9 14.8 %reshape.113 = bf16[16,1024,2,64]{3,2,1,0:T(2,128)(2,1)} reshape(bf16[64,256,128]{2,1,0:T(8,128)(2,1)} %get-tuple-element.124) | data formatting | bytes 8388608 | tf_op jit(solution)/shard_map/reshape;reshape | solution.py:137
  328.7 20.1 %copy.75 = bf16[16,1024,2,64]{1,3,2,0:T(8,128)(2,1)} copy(bf16[16,1024,2,64]{3,2,1,0:T(2,128)(2,1)} %reshape.113) | data formatting | bytes 8388608
  348.8 14.7 %reshape.112 = bf16[16,1024,2,64]{3,2,1,0:T(2,128)(2,1)} reshape(bf16[64,256,128]{2,1,0:T(8,128)(2,1)} %get-tuple-element.125) | data formatting | bytes 8388608 | tf_op jit(solution)/shard_map/reshape;reshape | solution.py:136
  363.6 20.1 %copy.74 = bf16[16,1024,2,64]{1,3,2,0:T(8,128)(2,1)} copy(bf16[16,1024,2,64]{3,2,1,0:T(2,128)(2,1)} %reshape.112) | data formatting | bytes 8388608
  383.7 58.0 %while.15 = (s32[]{:T(128)}, f32[2,256]{1,0:T(2,128)S(1)}, f32[2,256]{1,0:T(2,128)S(1)}, f32[2,256,64]{1,2,0:T(8,128)S(1)}, bf16[16,1024,2,64]{1,3,2,0:T(8,128)(...) while((s32[]{:T(128)}, f32[2,256]{1,0:T(2,128)S(1)}, ...), condition=%wide.region_5.6_spmd.clone, body=%wide.region_2.5_spmd.clone.sunk | while | flops 140085760 | bytes 7196805 | solution.py:140
  383.7 1.5 bitcast_reduce_fusion.2
  385.7 1.6 convolution_add_fusion.3
  387.3 1.5 bitcast_reduce_fusion.2
  389.3 1.6 convolution_add_fusion.3
  390.9 1.5 bitcast_reduce_fusion.2
  392.9 1.6 convolution_add_fusion.3
  394.5 1.5 bitcast_reduce_fusion.2
  396.6 1.6 convolution_add_fusion.3
  398.2 1.5 bitcast_reduce_fusion.2
  400.2 1.6 convolution_add_fusion.3
  401.8 1.5 bitcast_reduce_fusion.2
  403.8 1.6 convolution_add_fusion.3
  405.4 1.5 bitcast_reduce_fusion.2
  407.4 1.6 convolution_add_fusion.3
  409.1 1.5 bitcast_reduce_fusion.2
  411.1 1.6 convolution_add_fusion.3
  412.7 1.5 bitcast_reduce_fusion.2
  414.7 1.6 convolution_add_fusion.3
  416.3 1.5 bitcast_reduce_fusion.2
  418.3 1.6 convolution_add_fusion.3
  420.0 1.5 bitcast_reduce_fusion.2
  422.0 1.6 convolution_add_fusion.3
  423.6 1.5 bitcast_reduce_fusion.2
  425.6 1.6 convolution_add_fusion.3
  427.2 1.5 bitcast_reduce_fusion.2
  429.2 1.6 convolution_add_fusion.3
  430.8 1.5 bitcast_reduce_fusion.2
  432.8 1.6 convolution_add_fusion.3
  434.5 1.5 bitcast_reduce_fusion.2
  436.5 1.6 convolution_add_fusion.3
  438.1 1.5 bitcast_reduce_fusion.2
  440.1 1.6 convolution_add_fusion.3
  441.7 12.4 %all_gather.7 = bf16[256,512]{0,1:T(8,128)(2,1)S(1)} all-gather(bf16[256,128]{0,1:T(8,128)(2,1)S(1)} %bitcast.107), channel_id=1, replica_groups=mesh['space'=64,'head'=4] {'head'}, dimensions={1}, use_global_device_ids=true | all-gather | bytes 327680 | tf_op jit(solution)/shard_map/all_gather | solution.py:149
  454.1 0.9 fusion.39
  (132 shorter events, 13.3 us)
Async XLA Ops:
  0.6 91.1 %copy-start = (bf16[8,128,512]{2,1,0:T(8,128)(2,1)S(1)}, bf16[8,128,512]{2,1,0:T(8,128)(2,1)}, u32[]{:S(2)}) copy-start(bf16[8,128,512]{2,1,0:T(8,128)(2,1)} %param.14) | copy-start | bytes 3145732
  4.5 3.1 collective-permute-start
  6.2 4.5 collective-permute-start.1
  61.5 1.2 copy-start.5
  61.6 1.2 copy-start.7
  68.9 6.9 %copy-start.3 = (bf16[128,512]{1,0:T(8,128)(2,1)S(1)}, bf16[128,512]{1,0:T(8,128)(2,1)}, u32[]{:S(2)}) copy-start(bf16[128,512]{1,0:T(8,128)(2,1)} %param.17) | copy-start | bytes 393220
  68.9 12.2 %copy-start.2 = (s32[8,16,16]{2,1,0:T(8,128)S(1)}, s32[8,16,16]{2,1,0:T(8,128)}, u32[]{:S(2)}) copy-start(s32[8,16,16]{2,1,0:T(8,128)} %param.11) | copy-start | bytes 24580
  70.2 13.0 %collective-permute-start.2 = (bf16[1,16,16,128]{3,1,2,0:T(8,128)(2,1)}, bf16[1,16,16,128]{3,1,2,0:T(8,128)(2,1)S(1)}, u32[]{:S(2)}, u32[]{:S(2)}) collective-permute-start(bf16[1,16,16,128]{3,1,2,0:T(8,128)(2,1)} %get-tuple-element.128), channel_id=1, source_target_pairs={{0,4},{4,8},{8,12},{12,16},{16,20},{20,24},{24,28},{28,32},{32,36}... | collective-permute-start | bytes 196616 | tf_op jit(solution)/shard_map/ppermute | solution.py:17
  74.5 8.7 %collective-permute-start.3 = (bf16[1,16,16,128]{3,1,2,0:T(8,128)(2,1)S(1)}, bf16[1,16,16,128]{3,1,2,0:T(8,128)(2,1)S(1)}, u32[]{:S(2)}, u32[]{:S(2)}) collective-permute-start(bf16[1,16,16,128]{3,1,2,0:T(8,128)(2,1)S(1)} %get-tuple-element.129), channel_id=1, source_target_pairs={{4,0},{8,4},{12,8},{16,12},{20,16},{24,20},{28,24},{32,28},{36,32}... | collective-permute-start | bytes 196616 | tf_op jit(solution)/shard_map/ppermute | solution.py:19
  76.6 16.3 %all-to-all-start.1 = ((bf16[128,4,128]{0,2,1:T(8,128)(2,1)}), bf16[128,4,128]{0,2,1:T(8,128)(2,1)S(1)}, u32[]{:S(2)}, u32[]{:S(2)}) async-start(bf16[128,4,128]{0,2,1:T(8,128)(2,1)} %bitcast.24), calls=%async_computation.1 | async-start | bytes 262144 | tf_op jit(solution)/shard_map/all_to_all | solution.py:148
  83.3 1.2 copy-start.6
  83.3 1.2 copy-start.8
  91.3 0.9 copy-start.4
  96.8 210.0 %all-to-all-start = ((bf16[64,1,264,256]{3,2,1,0:T(8,128)(2,1)}), bf16[64,1,264,256]{3,2,1,0:T(8,128)(2,1)}, u32[]{:S(2)}, u32[]{:S(2)}) async-start(bf16[64,1,264,256]{3,2,1,0:T(8,128)(2,1)} %stack.3), calls=%async_computation | async-start | bytes 17301504 | tf_op jit(solution)/shard_map/all_to_all | solution.py:96
  441.7 13.3 %copy-start.1 = (bf16[8,128,512]{2,1,0:T(8,128)(2,1)S(1)}, bf16[8,128,512]{2,1,0:T(8,128)(2,1)}, u32[]{:S(2)}) copy-start(bf16[8,128,512]{2,1,0:T(8,128)(2,1)} %param.14) | copy-start | bytes 3145732
